TPU v7x, 512 devices: a whole 4x8x8 slice. The times are simulated.
512 devices in a mesh: ctx: 16 (over y, x_hi), tp: 32 (over z, x_lo, core).
Axes of the slice: x: 4 (x_hi: 2, x_lo: 2; x = x_hi * 2 + x_lo), y: 8, z: 8, core: 2. Of those that a mesh axis runs over, the one named last changes fastest.
Arguments:
- resid_in: bfloat16 [2048, 4096], P('ctx', 'tp'), may hold values from -6 to 6
- feats: bfloat16 [2048, 3, 4096], P('ctx', None, 'tp'), may hold values from -6 to 6
- short_filter: float32 [3, 3, 4096], P(None, None, 'tp'), may hold values from -3.5 to 3.5
- residues: float32 [4096, 16], P('tp'), may hold values from -4 to 4
- rates: float32 [4096, 16], P('tp'), may hold values from 0.00014648438 to 0.03
- out_weight: bfloat16 [4096, 4096], P('tp'), may hold values from -0.1875 to 0.1875
- norm_gain: float32 [4096], replicated, may hold values from 0.1 to 1.9
- attn_weight: bfloat16 [4096, 3, 4096], P(None, None, 'tp'), may hold values from -1 to 1
Outputs:
- hyena_out: bfloat16 [2048, 4096], P('ctx', 'tp')
- context: bfloat16 [2048, 4096], P('ctx', 'tp')
All inputs are finite; a program needn't handle non-finite values.
Results may differ from a plain program's by a relative error of at most 0.01.
Values may be sent and summed in bfloat16 or wider, within the bound.
No kernel may reach another device: no remote copies, remote signals or barrier semaphores. Data moves between devices by JAX's collectives and lax.ppermute only.
A program may use at most 192 MiB of HBM per device.

v0:
```python
import math
import jax
import jax.numpy as jnp
from jax import lax
from jax.sharding import PartitionSpec as P

HEAD_DIM = 128
eps_norm = 1e-05
rope_base = 10000.0
mask_fill = -1e30
highest = lax.Precision.HIGHEST


def shifted(value, axis, steps):
    count = lax.axis_size(axis)
    initial, last = (max(0, -steps), min(count, count - steps))
    return lax.ppermute(value, axis, [(source, source + steps) for source in range(initial, last)])


def toeplitz_lower(filter_taps):
    chan_count, block_size = filter_taps.shape
    padded = jnp.concatenate(
        [jnp.zeros((chan_count, block_size - 1), jnp.float32), filter_taps], axis=1
    )
    flipped = padded[:, ::-1]
    tiled = jnp.tile(flipped, (1, block_size))
    offset = block_size - 1
    window = tiled[:, offset : offset + block_size * (2 * block_size - 2)]
    return window.reshape(chan_count, block_size, 2 * block_size - 2)[:, :, :block_size]


def modal_conv(signal, residues, rates, start_state):
    chan_count, length = signal.shape
    block_size = math.gcd(length, 128)
    block_count = length // block_size
    weight = residues * jnp.sqrt(1.0 - jnp.exp(-2.0 * rates))
    lag_steps = jnp.arange(block_size, dtype=jnp.float32)
    powers = jnp.exp(-rates[:, :, None] * lag_steps)
    filter_taps = jnp.sum(weight[:, :, None] * powers, axis=1)
    toeplitz = toeplitz_lower(filter_taps)
    blocks = signal.reshape(chan_count, block_count, block_size)
    inner_part = jnp.einsum("cij,cnj->cni", toeplitz, blocks, precision=highest)
    tail_powers = jnp.exp(-rates[:, :, None] * (block_size - lag_steps))
    end_states = jnp.einsum("cnj,cmj->cnm", blocks, tail_powers, precision=highest)
    block_steps = jnp.arange(block_count, dtype=jnp.float32)
    gap_count = block_steps[:, None] - 1.0 - block_steps[None, :]
    live_mask = gap_count >= 0.0
    carry_mat = jnp.where(
        live_mask, jnp.exp(-rates[:, :, None, None] * block_size * jnp.maximum(gap_count, 0.0)), 0.0
    )
    states = jnp.einsum("cmnk,ckm->cnm", carry_mat, end_states, precision=highest)
    states = (
        states
        + jnp.exp(-rates[:, None, :] * block_size * block_steps[None, :, None])
        * start_state[:, None, :]
    )
    cross_part = jnp.einsum("cnm,cmi->cni", states * weight[:, None, :], powers, precision=highest)
    return (inner_part + cross_part).reshape(chan_count, length)


def short_mix(feats, short_filter):
    row_count = feats.shape[0]
    prior_feats = shifted(feats[-2:], "ctx", 1)
    joined = jnp.concatenate([prior_feats, feats], axis=0).astype(jnp.float32)
    return (
        short_filter[0] * joined[2:]
        + short_filter[1] * joined[1 : row_count + 1]
        + short_filter[2] * joined[:row_count]
    )


def rotary_turn(vectors, positions):
    half_dim = vectors.shape[-1] // 2
    frequency = rope_base ** (-jnp.arange(half_dim, dtype=jnp.float32) * 2.0 / vectors.shape[-1])
    angles = positions.astype(jnp.float32)[:, None] * frequency[None, :]
    cosine = jnp.cos(angles)[:, None, :]
    sine_part = jnp.sin(angles)[:, None, :]
    first_half = vectors[..., :half_dim]
    second = vectors[..., half_dim:]
    return jnp.concatenate(
        [first_half * cosine - second * sine_part, second * cosine + first_half * sine_part],
        axis=-1,
    )


def attend_tile(running, query_rows, query_pos, key_block, value_block, key_start):
    run_peak, denom, accumulated = running
    block_size = key_block.shape[0]
    score_scale = 1.0 / math.sqrt(key_block.shape[2])
    key_pos = key_start + jnp.arange(block_size, dtype=jnp.int32)
    scores = (
        jnp.einsum("shd,khd->hsk", query_rows, key_block, preferred_element_type=jnp.float32)
        * score_scale
    )
    allowed = (query_pos[:, None] >= key_pos[None, :])[None]
    masked = jnp.where(allowed, scores, mask_fill)
    new_peak = jnp.maximum(run_peak, jnp.max(masked, axis=2))
    weights = jnp.where(allowed, jnp.exp(masked - new_peak[:, :, None]), 0.0)
    factor = jnp.exp(run_peak - new_peak)
    denom = denom * factor + jnp.sum(weights, axis=2)
    accumulated = accumulated * factor[:, :, None] + jnp.einsum(
        "hsk,khd->hsd",
        weights.astype(jnp.bfloat16),
        value_block,
        preferred_element_type=jnp.float32,
    )
    return (new_peak, denom, accumulated)


def empty_state(head_count, rows):
    return (
        jnp.full((head_count, rows), mask_fill, jnp.float32),
        jnp.zeros((head_count, rows), jnp.float32),
        jnp.zeros((head_count, rows, HEAD_DIM), jnp.float32),
    )


def finish_rows(state):
    run_peak, denom, accumulated = state
    heads_out = accumulated / denom[:, :, None]
    rows = heads_out.shape[1]
    return (
        heads_out.transpose(1, 0, 2)
        .reshape(rows, heads_out.shape[0] * heads_out.shape[2])
        .astype(jnp.bfloat16)
    )


def per_device(resid_in, feats, short_filter, residues, rates, out_weight, norm_gain, attn_weight):
    row_count, chan_count = resid_in.shape
    width_all = out_weight.shape[1]
    short_out = short_mix(feats, short_filter)
    product = (short_out[:, 1] * short_out[:, 2]).astype(jnp.bfloat16)
    panel_rows = lax.all_to_all(product.T, "ctx", split_axis=0, concat_axis=1, tiled=True)
    panel_count = chan_count // lax.axis_size("ctx")
    panel_start = lax.axis_index("ctx") * panel_count
    panel_res = lax.dynamic_slice_in_dim(residues, panel_start, panel_count, 0)
    panel_rates = lax.dynamic_slice_in_dim(rates, panel_start, panel_count, 0)
    panel_conv = modal_conv(
        panel_rows.astype(jnp.float32), panel_res, panel_rates, jnp.zeros_like(panel_rates)
    )
    returned = lax.all_to_all(panel_conv, "ctx", split_axis=1, concat_axis=0, tiled=True)
    conv_out = returned.T
    gated = (short_out[:, 0] * conv_out).astype(jnp.bfloat16)
    own_share = lax.psum_scatter(
        lax.dot_general(
            out_weight, gated, (((0,), (1,)), ((), ())), preferred_element_type=jnp.float32
        ),
        "tp",
        scatter_dimension=0,
        tiled=True,
    )
    hyena_out = (resid_in.astype(jnp.float32) + own_share.T).astype(jnp.bfloat16)
    full_rows = lax.all_gather(hyena_out, "tp", axis=1, tiled=True)
    wide = full_rows.astype(jnp.float32)
    mean_square = jnp.mean(wide * wide, axis=1, keepdims=True)
    normed = (wide * lax.rsqrt(mean_square + eps_norm) * norm_gain).astype(jnp.bfloat16)
    projected = jnp.dot(
        normed, attn_weight.reshape(width_all, 3 * chan_count), preferred_element_type=jnp.float32
    ).reshape(row_count, 3, chan_count)
    head_count = chan_count // HEAD_DIM
    ctx_index = lax.axis_index("ctx")
    first_pos = ctx_index * row_count
    positions = first_pos + jnp.arange(row_count, dtype=jnp.int32)
    queries = rotary_turn(
        projected[:, 0].reshape(row_count, head_count, HEAD_DIM), positions
    ).astype(jnp.bfloat16)
    keys_all = rotary_turn(
        projected[:, 1].reshape(row_count, head_count, HEAD_DIM), positions
    ).astype(jnp.bfloat16)
    values = projected[:, 2].astype(jnp.bfloat16)
    key_pieces = (keys_all.reshape(row_count, chan_count), values)
    initial = empty_state(head_count, row_count)
    key_rows = lax.all_gather(key_pieces[0], "ctx", axis=0, tiled=True)
    value_rows = lax.all_gather(key_pieces[1], "ctx", axis=0, tiled=True)
    key_total = key_rows.shape[0]
    tiles_block_size = math.gcd(key_total, 1024)
    block_count = key_total // tiles_block_size
    key_blocks = key_rows.reshape(block_count, tiles_block_size, head_count, HEAD_DIM)
    value_blocks = value_rows.reshape(block_count, tiles_block_size, head_count, HEAD_DIM)
    key_blocks, value_blocks, block_ids, block_size = (
        key_blocks,
        value_blocks,
        jnp.arange(block_count, dtype=jnp.int32),
        tiles_block_size,
    )

    def one_tile(carried, slot_item):
        key_block, value_block, block_index = slot_item
        key_start = block_index * block_size
        updated = attend_tile(carried, queries, positions, key_block, value_block, key_start)
        return (updated, None)

    result, _ = lax.scan(one_tile, initial, (key_blocks, value_blocks, block_ids))
    context = finish_rows(result)
    return (hyena_out, context)


def solution(mesh):
    in_specs = (
        P("ctx", "tp"),
        P("ctx", None, "tp"),
        P(None, None, "tp"),
        P("tp", None),
        P("tp", None),
        P("tp", None),
        P(),
        P(None, None, "tp"),
    )
    out_specs = (P("ctx", "tp"), P("ctx", "tp"))
    return jax.shard_map(
        per_device, mesh=mesh, in_specs=in_specs, out_specs=out_specs, check_vma=False
    )
```

profile of v0, /device:TPU:4, one launch (start us, length us, event | category | flops | bytes accessed | tf_op | source)
XLA Modules:
  0.0 341.5 jit_solution(16704651836069771264)
XLA Ops:
  7.2 0.8 slice.59
  8.1 3.4 %collective-permute-start = (bf16[2,3,128]{0,2,1:T(8,128)(2,1)S(1)}, bf16[2,3,128]{0,2,1:T(8,128)(2,1)S(1)}, u32[]{:S(2)}, u32[]{:S(2)}) collective-permute-start(bf16[2,3,128]{0,2,1:T(8,128)(2,1)S(1)} %copy.44), channel_id=1, source_target_pairs={{0,32},{32,64},{64,96},{96,128},{128,160},{160,192},{192,224},{224... | collective-permute-start | bytes 4616 | tf_op jit(solution)/shard_map/ppermute | solution.py:17
  11.8 0.8 constant_dynamic-slice_fusion
  12.7 0.7 slice_bitcast_fusion.3
  13.5 1.0 copy.45
  14.9 0.6 tile.10
  15.5 0.3 slice.81
  15.9 1.6 reshape.257
  17.5 0.4 collective-permute-done
  18.4 0.6 fusion.65
  19.0 8.8 %all-to-all-start = ((bf16[16,8,128]{2,1,0:T(8,128)(2,1)}), bf16[16,8,128]{2,1,0:T(8,128)(2,1)S(1)}, u32[]{:S(2)}, u32[]{:S(2)}) async-start(bf16[16,8,128]{2,1,0:T(8,128)(2,1)} %fusion.65), calls=%async_computation | async-start | bytes 65536 | tf_op jit(solution)/shard_map/all_to_all | solution.py:134
  27.8 7.4 %all-to-all-done = bf16[16,8,128]{2,1,0:T(8,128)(2,1)S(1)} async-done(((bf16[16,8,128]{2,1,0:T(8,128)(2,1)}), bf16[16,8,128]{2,1,0:T(8,128)(2,1)S(1)}, u32[]{:S(2)}, u32[]{:S(2)}) %all-to-all-start) | async-done | bytes 32800 | tf_op jit(solution)/shard_map/all_to_all | solution.py:134
  35.5 0.6 multiply_reduce_fusion
  36.2 0.5 fusion.32
  37.0 13.1 %all_to_all.32 = f32[8,16,128]{2,0,1:T(8,128)S(1)} all-to-all(f32[8,16,128]{2,0,1:T(8,128)S(1)} %copy.49), channel_id=1, replica_groups=mesh['ctx'=16,'tp'=32] {'ctx'}, dimensions={1} | all-to-all | bytes 131072 | tf_op jit(solution)/shard_map/all_to_all | solution.py:142
  50.2 1.8 convolution_bitcast_fusion.1
  52.1 122.4 %reduce-scatter.2.cloned.1.call-done = f32[128,128]{0,1:T(8,128)} async-done(((f32[4096,128]{0,1:T(8,128)}), f32[128,128]{0,1:T(8,128)}) %reduce-scatter.2.cloned.1.call-update) | async-done | bytes 65552 | tf_op jit(solution)/shard_map/reduce_scatter | solution.py:145
  174.4 1.5 fusion.39
  176.0 4.7 %copy.50 = bf16[4096,3,128]{0,2,1:T(8,128)(2,1)} copy(bf16[4096,3,128]{2,0,1:T(8,128)(2,1)} %param.17) | data formatting | bytes 6291456 | tf_op args[7]
  180.7 59.4 %all-gather.3.cloned.1.call-done = bf16[128,4096]{1,0:T(8,128)(2,1)} async-done(((bf16[128,128]{1,0:T(8,128)(2,1)}), bf16[128,4096]{1,0:T(8,128)(2,1)}) %all-gather.3.cloned.1.call-update) | async-done | bytes 1048592 | tf_op jit(solution)/shard_map/all_gather | solution.py:154
  240.1 1.5 fusion.25
  241.6 3.3 fusion.23
  245.3 39.5 %all_gather.10 = bf16[2048,128]{0,1:T(8,128)(2,1)S(1)} all-gather(bf16[128,128]{0,1:T(8,128)(2,1)S(1)} %pad_maximum_fusion), channel_id=1, replica_groups=mesh['ctx'=16,'tp'=32] {'ctx'}, dimensions={0}, use_global_device_ids=true | all-gather | bytes 557056 | tf_op jit(solution)/shard_map/all_gather | solution.py:174
  285.0 44.0 %all-gather = bf16[2048,1,128]{0,2,1:T(8,128)(2,1)S(1)} all-gather(bf16[128,1,128]{0,2,1:T(8,128)(2,1)S(1)} %slice.136), channel_id=2, replica_groups=mesh['ctx'=16,'tp'=32] {'ctx'}, dimensions={0}, use_global_device_ids=true | all-gather | bytes 557056 | tf_op jit(solution)/shard_map/all_gather | solution.py:175
  329.3 4.6 %while.15 = (s32[]{:T(128)}, f32[1,128]{1,0:T(1,128)S(1)}, f32[1,128]{1,0:T(1,128)S(1)}, f32[1,128,128]{2,1,0:T(8,128)S(1)}, s32[2]{0:T(128)S(1)}, /*index=5*/bf...) while((s32[]{:T(128)}, f32[1,128]{1,0:T(1,128)S(1)}, ...), condition=%wide.region_6.7_spmd.clone, body=%wide.region_3.6_spmd.clone.sunk | while | flops 68732800 | bytes 2287785 | solution.py:194
  329.3 0.6 dynamic_slice.39
  330.6 0.3 fusion.93
  330.9 0.4 fusion.97
  331.6 0.6 dynamic_slice.39
  332.9 0.3 fusion.93
  333.3 0.4 fusion.97
  333.9 0.7 fusion.74
  (56 shorter events, 3.7 us)
Async XLA Ops:
  7.2 43.0 %copy-start = (bf16[128,4096]{1,0:T(8,128)(2,1)S(1)}, bf16[128,4096]{1,0:T(8,128)(2,1)}, u32[]{:S(2)}) copy-start(bf16[128,4096]{1,0:T(8,128)(2,1)} %param.15) | copy-start | bytes 3145732
  8.1 9.7 %collective-permute-start = (bf16[2,3,128]{0,2,1:T(8,128)(2,1)S(1)}, bf16[2,3,128]{0,2,1:T(8,128)(2,1)S(1)}, u32[]{:S(2)}, u32[]{:S(2)}) collective-permute-start(bf16[2,3,128]{0,2,1:T(8,128)(2,1)S(1)} %copy.44), channel_id=1, source_target_pairs={{0,32},{32,64},{64,96},{96,128},{128,160},{160,192},{192,224},{224... | collective-permute-start | bytes 4616 | tf_op jit(solution)/shard_map/ppermute | solution.py:17
  19.0 16.2 %all-to-all-start = ((bf16[16,8,128]{2,1,0:T(8,128)(2,1)}), bf16[16,8,128]{2,1,0:T(8,128)(2,1)S(1)}, u32[]{:S(2)}, u32[]{:S(2)}) async-start(bf16[16,8,128]{2,1,0:T(8,128)(2,1)} %fusion.65), calls=%async_computation | async-start | bytes 65536 | tf_op jit(solution)/shard_map/all_to_all | solution.py:134
  27.8 146.7 %reduce-scatter.2.cloned.1.call-start = ((), (), s32[]{:S(2)}) async-start(), calls=%async_computation.3 | async-start | bytes 2162688 | tf_op jit(solution)/shard_map/reduce_scatter | solution.py:145
  50.2 124.3 %copy-start.1 = (bf16[128,128]{1,0:T(8,128)(2,1)S(1)}, bf16[128,128]{1,0:T(8,128)(2,1)}, u32[]{:S(2)}) copy-start(bf16[128,128]{1,0:T(8,128)(2,1)} %param.10) | copy-start | bytes 98308
  52.0 188.1 %all-gather.3.cloned.1.call-start = ((), (), s32[]{:S(2)}) async-start(), calls=%async_computation.4 | async-start | bytes 1081344 | tf_op jit(solution)/shard_map/all_gather | solution.py:154
  175.9 65.7 %copy-start.2 = (f32[4096]{0:T(1024)S(1)}, f32[4096]{0:T(1024)}, u32[]{:S(2)}) copy-start(f32[4096]{0:T(1024)} %param.16) | copy-start | bytes 49156
Sparse Core Ops, SparseCore 0:
  52.1 122.2 reduce-scatter.1
  177.3 62.7 all-gather.2
where the time goes:
time: 342 us; the launch traced here: 341 us
  waiting for transfers between devices  190 us (56%)
  blocking collectives  96.6 us (28%)
  between operations  14.3 us (4%)
  local copies, waits for them, and re-layouts  13.3 us (4%)
  starting transfers between devices  12.3 us (4%)
  matrix products  7.62 us (2%)
  other arithmetic  6.38 us (2%)
    reduce_scatter x1, waiting for transfers between devices, per_device(): lax.psum_scatter(lax.dot_general(out_weight, gated, (((0,), (1,)), ((), (...  122 us
    all_gather x1, waiting for transfers between devices, per_device(): full_rows = lax.all_gather(hyena_out, 'tp', axis=1, tiled=True)  59.4 us
    all_gather x1, blocking collectives, per_device(): value_rows = lax.all_gather(key_pieces[1], 'ctx', axis=0, tiled=True)  44 us
    all_gather x1, blocking collectives, per_device(): key_rows = lax.all_gather(key_pieces[0], 'ctx', axis=0, tiled=True)  39.5 us
    all_to_all x1, blocking collectives, per_device(): lax.all_to_all(panel_conv, 'ctx', split_axis=1, concat_axis=0, tiled=True)  13.1 us
    all_to_all x1, starting transfers between devices, per_device(): lax.all_to_all(product.T, 'ctx', split_axis=0, concat_axis=1, tiled=True)  8.78 us
    all_to_all x1, waiting for transfers between devices, per_device(): lax.all_to_all(product.T, 'ctx', split_axis=0, concat_axis=1, tiled=True)  7.39 us
  transfers between devices with their start and end apart: 4, of which 4 were waited for; matrix products, arithmetic and copies ran while one was open for 3% of the time, Pallas kernels for 0%

commit v1 on v0

--- a/solution.py
+++ b/solution.py
@@ -171,7 +171,9 @@
     values = projected[:, 2].astype(jnp.bfloat16)
     key_pieces = (keys_all.reshape(row_count, chan_count), values)
     initial = empty_state(head_count, row_count)
-    key_rows = lax.all_gather(key_pieces[0], "ctx", axis=0, tiled=True)
+    key_rows = jnp.concatenate(
+        lax.all_to_all(jnp.stack([key_pieces[0]] * lax.axis_size("ctx")), "ctx", 0, 0), axis=0
+    )
     value_rows = lax.all_gather(key_pieces[1], "ctx", axis=0, tiled=True)
     key_total = key_rows.shape[0]
     tiles_block_size = math.gcd(key_total, 1024)

time: 342 us -> 317 us (0.927)
  the two profiles are of different devices: /device:TPU:4 before, /device:TPU:32 now
where the time goes in v1:
time: 317 us
  waiting for transfers between devices  189 us (60%)
  blocking collectives  62 us (20%)
  starting transfers between devices  21.8 us (7%)
  between operations  14.3 us (5%)
  local copies, waits for them, and re-layouts  14.1 us (4%)
  matrix products  7.61 us (2%)
  other arithmetic  6.38 us (2%)
    reduce_scatter x1, waiting for transfers between devices, per_device(): lax.psum_scatter(lax.dot_general(out_weight, gated, (((0,), (1,)), ((), (...  125 us
    all_gather x1, waiting for transfers between devices, per_device(): full_rows = lax.all_gather(hyena_out, 'tp', axis=1, tiled=True)  59.5 us
    all_gather x1, blocking collectives, per_device(): value_rows = lax.all_gather(key_pieces[1], 'ctx', axis=0, tiled=True)  48.8 us
    all_to_all x1, blocking collectives, per_device(): lax.all_to_all(panel_conv, 'ctx', split_axis=1, concat_axis=0, tiled=True)  13.2 us
    all_to_all x1, starting transfers between devices, per_device(): lax.all_to_all(jnp.stack([key_pieces[0]] * lax.axis_size('ctx')), 'ctx',...  9.51 us
    all_to_all x1, starting transfers between devices, per_device(): lax.all_to_all(product.T, 'ctx', split_axis=0, concat_axis=1, tiled=True)  7.28 us
    unnamed x15, local copies, waits for them, and re-layouts  6.55 us
  transfers between devices with their start and end apart: 5, of which 3 were waited for; matrix products, arithmetic and copies ran while one was open for 3% of the time, Pallas kernels for 0%

profile of v1, /device:TPU:32, one launch (start us, length us, event | category | flops | bytes accessed | tf_op | source)
XLA Modules:
  0.0 316.8 jit_solution(1004326427091582723)
XLA Ops:
  7.2 0.8 slice.59
  8.1 4.9 %collective-permute-start = (bf16[2,3,128]{0,2,1:T(8,128)(2,1)S(1)}, bf16[2,3,128]{0,2,1:T(8,128)(2,1)S(1)}, u32[]{:S(2)}, u32[]{:S(2)}) collective-permute-start(bf16[2,3,128]{0,2,1:T(8,128)(2,1)S(1)} %copy.46), channel_id=1, source_target_pairs={{0,32},{32,64},{64,96},{96,128},{128,160},{160,192},{192,224},{224... | collective-permute-start | bytes 4616 | tf_op jit(solution)/shard_map/ppermute | solution.py:17
  13.3 0.8 constant_dynamic-slice_fusion
  14.2 0.7 slice_bitcast_fusion.3
  15.0 1.0 copy.47
  16.4 0.6 tile.10
  17.0 0.3 slice.81
  17.4 1.6 reshape.258
  19.5 0.6 fusion.65
  20.1 7.3 %all-to-all-start = ((bf16[16,8,128]{2,1,0:T(8,128)(2,1)}), bf16[16,8,128]{2,1,0:T(8,128)(2,1)S(1)}, u32[]{:S(2)}, u32[]{:S(2)}) async-start(bf16[16,8,128]{2,1,0:T(8,128)(2,1)} %fusion.65), calls=%async_computation | async-start | bytes 65536 | tf_op jit(solution)/shard_map/all_to_all | solution.py:134
  27.4 5.0 %all-to-all-done = bf16[16,8,128]{2,1,0:T(8,128)(2,1)S(1)} async-done(((bf16[16,8,128]{2,1,0:T(8,128)(2,1)}), bf16[16,8,128]{2,1,0:T(8,128)(2,1)S(1)}, u32[]{:S(2)}, u32[]{:S(2)}) %all-to-all-start) | async-done | bytes 32800 | tf_op jit(solution)/shard_map/all_to_all | solution.py:134
  32.8 0.6 multiply_reduce_fusion
  33.4 0.5 fusion.32
  34.3 13.2 %all_to_all.37 = f32[8,16,128]{2,0,1:T(8,128)S(1)} all-to-all(f32[8,16,128]{2,0,1:T(8,128)S(1)} %copy.51), channel_id=1, replica_groups=mesh['ctx'=16,'tp'=32] {'ctx'}, dimensions={1} | all-to-all | bytes 131072 | tf_op jit(solution)/shard_map/all_to_all | solution.py:142
  47.5 1.8 convolution_bitcast_fusion.1
  49.3 124.8 %reduce-scatter.2.cloned.1.call-done = f32[128,128]{0,1:T(8,128)} async-done(((f32[4096,128]{0,1:T(8,128)}), f32[128,128]{0,1:T(8,128)}) %reduce-scatter.2.cloned.1.call-update) | async-done | bytes 65552 | tf_op jit(solution)/shard_map/reduce_scatter | solution.py:145
  174.1 1.5 fusion.39
  175.6 4.7 %copy.52 = bf16[4096,3,128]{0,2,1:T(8,128)(2,1)} copy(bf16[4096,3,128]{2,0,1:T(8,128)(2,1)} %param.17) | data formatting | bytes 6291456 | tf_op args[7]
  180.3 59.5 %all-gather.3.cloned.1.call-done = bf16[128,4096]{1,0:T(8,128)(2,1)} async-done(((bf16[128,128]{1,0:T(8,128)(2,1)}), bf16[128,4096]{1,0:T(8,128)(2,1)}) %all-gather.3.cloned.1.call-update) | async-done | bytes 1048592 | tf_op jit(solution)/shard_map/all_gather | solution.py:154
  239.9 1.5 fusion.25
  241.4 3.3 %fusion.23 = f32[128,3,128]{0,2,1:T(8,128)S(1)} fusion(bf16[4096,3,128]{0,2,1:T(8,128)(2,1)} %copy.52, bf16[128,4096]{1,0:T(8,128)(2,1)} %all-gather.3.cloned.1.call-done, f32[4096]{0:T(1024)S(1)} %copy-done.2, f32[128]{0:T(128)S(1)} %add_rsqrt_fusion), kind=kOutput, calls=%fused_computation.32 | convolution fusion | flops 404750336 | bytes 4407808 | tf_op jit(solution)/shard_map/dot_general | solution.py:158
  245.0 0.9 stack.3
  245.9 9.5 %all-to-all-start.2 = ((bf16[16,128,128]{2,1,0:T(8,128)(2,1)}), bf16[16,128,128]{2,1,0:T(8,128)(2,1)S(1)}, u32[]{:S(2)}, u32[]{:S(2)}) async-start(bf16[16,128,128]{2,1,0:T(8,128)(2,1)} %stack.3), calls=%async_computation.3 | async-start | bytes 1048576 | tf_op jit(solution)/shard_map/all_to_all | solution.py:175
  255.5 48.8 %all-gather = bf16[2048,1,128]{0,2,1:T(8,128)(2,1)S(1)} all-gather(bf16[128,1,128]{0,2,1:T(8,128)(2,1)S(1)} %slice.136), channel_id=2, replica_groups=mesh['ctx'=16,'tp'=32] {'ctx'}, dimensions={0}, use_global_device_ids=true | all-gather | bytes 557056 | tf_op jit(solution)/shard_map/all_gather | solution.py:177
  304.7 4.6 %while.15 = (s32[]{:T(128)}, f32[1,128]{1,0:T(1,128)S(1)}, f32[1,128]{1,0:T(1,128)S(1)}, f32[1,128,128]{2,1,0:T(8,128)S(1)}, s32[2]{0:T(128)S(1)}, /*index=5*/bf...) while((s32[]{:T(128)}, f32[1,128]{1,0:T(1,128)S(1)}, ...), condition=%wide.region_6.7_spmd.clone, body=%wide.region_3.6_spmd.clone.sunk | while | flops 68732800 | bytes 2287785 | solution.py:196
  304.7 0.6 dynamic_slice.39
  305.9 0.3 fusion.93
  306.3 0.4 fusion.97
  307.0 0.6 dynamic_slice.39
  308.2 0.3 fusion.93
  308.6 0.4 fusion.97
  309.2 0.7 fusion.74
  (58 shorter events, 3.5 us)
Async XLA Ops:
  7.2 40.3 %copy-start = (bf16[128,4096]{1,0:T(8,128)(2,1)S(1)}, bf16[128,4096]{1,0:T(8,128)(2,1)}, u32[]{:S(2)}) copy-start(bf16[128,4096]{1,0:T(8,128)(2,1)} %param.15) | copy-start | bytes 3145732
  8.1 10.8 %collective-permute-start = (bf16[2,3,128]{0,2,1:T(8,128)(2,1)S(1)}, bf16[2,3,128]{0,2,1:T(8,128)(2,1)S(1)}, u32[]{:S(2)}, u32[]{:S(2)}) collective-permute-start(bf16[2,3,128]{0,2,1:T(8,128)(2,1)S(1)} %copy.46), channel_id=1, source_target_pairs={{0,32},{32,64},{64,96},{96,128},{128,160},{160,192},{192,224},{224... | collective-permute-start | bytes 4616 | tf_op jit(solution)/shard_map/ppermute | solution.py:17
  20.1 12.3 %all-to-all-start = ((bf16[16,8,128]{2,1,0:T(8,128)(2,1)}), bf16[16,8,128]{2,1,0:T(8,128)(2,1)S(1)}, u32[]{:S(2)}, u32[]{:S(2)}) async-start(bf16[16,8,128]{2,1,0:T(8,128)(2,1)} %fusion.65), calls=%async_computation | async-start | bytes 65536 | tf_op jit(solution)/shard_map/all_to_all | solution.py:134
  27.4 146.7 %reduce-scatter.2.cloned.1.call-start = ((), (), s32[]{:S(2)}) async-start(), calls=%async_computation.4 | async-start | bytes 2162688 | tf_op jit(solution)/shard_map/reduce_scatter | solution.py:145
  47.5 126.6 %copy-start.1 = (bf16[128,128]{1,0:T(8,128)(2,1)S(1)}, bf16[128,128]{1,0:T(8,128)(2,1)}, u32[]{:S(2)}) copy-start(bf16[128,128]{1,0:T(8,128)(2,1)} %param.10) | copy-start | bytes 98308
  49.3 190.6 %all-gather.3.cloned.1.call-start = ((), (), s32[]{:S(2)}) async-start(), calls=%async_computation.5 | async-start | bytes 1081344 | tf_op jit(solution)/shard_map/all_gather | solution.py:154
  175.6 65.8 %copy-start.2 = (f32[4096]{0:T(1024)S(1)}, f32[4096]{0:T(1024)}, u32[]{:S(2)}) copy-start(f32[4096]{0:T(1024)} %param.16) | copy-start | bytes 49156
  245.9 58.7 %all-to-all-start.2 = ((bf16[16,128,128]{2,1,0:T(8,128)(2,1)}), bf16[16,128,128]{2,1,0:T(8,128)(2,1)S(1)}, u32[]{:S(2)}, u32[]{:S(2)}) async-start(bf16[16,128,128]{2,1,0:T(8,128)(2,1)} %stack.3), calls=%async_computation.3 | async-start | bytes 1048576 | tf_op jit(solution)/shard_map/all_to_all | solution.py:175
Sparse Core Ops, SparseCore 0:
  49.4 124.6 reduce-scatter.1
  176.9 62.8 all-gather.2
